TPU v7x, 32 devices: a whole 2x2x4 slice. The times are simulated.
32 devices in a mesh: groups: 2 (over y), frames: 4 (over z), heads: 4 (over x, core).
Axes of the slice: x: 2, y: 2, z: 4, core: 2. Of those that a mesh axis runs over, the one named last changes fastest.
Arguments:
- query_heads: bfloat16 [16384, 896], P(('groups', 'frames'), 'heads'), parts along dimension 0, may hold values from -6 to 6
- key_heads: bfloat16 [16384, 896], P(('groups', 'frames'), 'heads'), parts along dimension 0, may hold values from -0.04 to 8
- value_heads: bfloat16 [16384, 896], P(('groups', 'frames'), 'heads'), parts along dimension 0, may hold values from -6 to 6
- residual: bfloat16 [16384, 2240], P(('groups', 'frames', 'heads')), parts along dimension 0, may hold values from -6 to 6
- out_proj: bfloat16 [896, 2240], P('frames'), may hold values from -0.1875 to 0.1875
- frame_gate: float32 [32, 2240], P(('groups', 'frames')), parts along dimension 0, may hold values from -4 to 4
Outputs:
- updated: bfloat16 [16384, 2240], P(('groups', 'frames', 'heads')), parts along dimension 0
There are 2 independent parts, one for each index of `groups`. A program takes and returns all parts, laid end to end along the dimension named above; an argument that names none is the same for every part. Nothing has to cross between parts.
All inputs are finite; a program needn't handle non-finite values.
Results may differ from a plain program's by a relative error of at most 0.0033.
Values may be sent and summed in bfloat16 or wider, within the bound.
No kernel may reach another device: no remote copies, remote signals or barrier semaphores. Data moves between devices by JAX's collectives and lax.ppermute only.
A program may use at most 64 MiB of HBM per device.

v0:
```python
import jax
import jax.numpy as jnp
from jax import lax
from jax.sharding import PartitionSpec as P

HD = 112
HEADS_DEV = 2
FRAME_TOK = 512
EPSILON = 1e-06


def per_device(query_heads, key_heads, value_heads, residual, out_proj, frame_gate):
    length = query_heads.shape[0]
    frames_here = length // FRAME_TOK
    block_shape = (frames_here, FRAME_TOK, HEADS_DEV, HD)
    query_pos = jnp.maximum(query_heads, 0).reshape(block_shape)
    key_pos = jnp.maximum(key_heads, 0).reshape(block_shape)
    value_frames = value_heads.reshape(block_shape)
    frame_state = jnp.einsum(
        "fthi,fthj->fhij", key_pos, value_frames, preferred_element_type=jnp.float32
    )
    frame_sum = jnp.sum(key_pos, axis=1, dtype=jnp.float32)
    own_state = jnp.sum(frame_state, axis=0)
    own_sum = jnp.sum(frame_sum, axis=0)
    position = lax.axis_index("frames")
    gathered = (
        lax.all_gather(own_state[None], "frames", axis=0, tiled=True),
        lax.all_gather(own_sum[None], "frames", axis=0, tiled=True),
    )
    pieces = gathered[0].shape[0]
    is_lower = jnp.arange(pieces, dtype=jnp.int32) < position
    state_part = jnp.sum(jnp.where(is_lower[:, None, None, None], gathered[0], 0.0), axis=0)
    sum_part = jnp.sum(jnp.where(is_lower[:, None, None], gathered[1], 0.0), axis=0)
    prefix_state = state_part[None] + jnp.cumsum(frame_state, axis=0)
    prefix_sum = sum_part[None] + jnp.cumsum(frame_sum, axis=0)
    state_round = prefix_state.astype(jnp.bfloat16)
    sum_round = prefix_sum.astype(jnp.bfloat16)
    numerator = jnp.einsum(
        "fthi,fhij->fthj", query_pos, state_round, preferred_element_type=jnp.float32
    )
    denominator = (
        jnp.einsum("fthi,fhi->fth", query_pos, sum_round, preferred_element_type=jnp.float32)
        + EPSILON
    )
    attended = (
        (numerator / denominator[..., None]).astype(jnp.bfloat16).reshape(length, HEADS_DEV * HD)
    )
    rows_here = residual.shape[0]
    head_pos = lax.axis_index("heads")
    row_frame = (head_pos * rows_here + jnp.arange(rows_here, dtype=jnp.int32)) // FRAME_TOK
    selector = (row_frame[:, None] == jnp.arange(frames_here, dtype=jnp.int32)[None, :]).astype(
        jnp.float32
    )
    gate_rows = jnp.dot(
        selector, frame_gate, precision=lax.Precision.HIGHEST, preferred_element_type=jnp.float32
    )
    token_rows = lax.all_to_all(attended, "heads", split_axis=0, concat_axis=1, tiled=True)
    projected = jnp.dot(
        token_rows,
        lax.all_gather(out_proj, "frames", axis=0, tiled=True),
        preferred_element_type=jnp.float32,
    )
    return (residual.astype(jnp.float32) + gate_rows * projected).astype(jnp.bfloat16)


def solution(mesh):
    in_specs = (
        P(("groups", "frames"), "heads"),
        P(("groups", "frames"), "heads"),
        P(("groups", "frames"), "heads"),
        P(("groups", "frames", "heads"), None),
        P("frames", None),
        P(("groups", "frames"), None),
    )
    out_specs = P(("groups", "frames", "heads"), None)
    return jax.shard_map(
        per_device, mesh=mesh, in_specs=in_specs, out_specs=out_specs, check_vma=False
    )
```

profile of v0, /device:TPU:0, one launch (start us, length us, event | category | flops | bytes accessed | tf_op | source)
XLA Modules:
  0.0 113.2 jit_solution(14616134283706953128)
XLA Ops:
  6.5 0.0 copy-start
  6.5 0.0 copy-start.1
  6.5 0.0 all-gather.3.cloned.1.call-start
  6.5 0.7 all-gather.3.cloned.1.call-update
  7.3 1.4 %convert_reduce_fusion.1 = f32[224]{0:T(256)S(1)} fusion(bf16[2048,224]{0,1:T(8,128)(2,1)} %param.7), kind=kLoop, calls=%fused_computation.6 | loop fusion | flops 1376032 | bytes 918400 | tf_op jit(solution)/shard_map/reduce_sum | solution.py:24
  8.7 0.1 broadcast_in_dim.41
  8.8 1.2 %broadcast_maximum_fusion = bf16[2048,224]{0,1:T(8,128)(2,1)S(1)} fusion(bf16[2048,224]{0,1:T(8,128)(2,1)} %param.6), kind=kLoop, calls=%fused_computation.16 | loop fusion | flops 458752 | bytes 1835008 | tf_op jit(solution)/shard_map/max | solution.py:16
  10.0 0.7 reshape.48
  10.7 3.2 %reshape.47 = bf16[4,512,2,112]{1,0,3,2:T(4,128)(2,1)} reshape(bf16[2048,224]{0,1:T(8,128)(2,1)} %param.8) | data formatting | bytes 1835008 | tf_op jit(solution)/shard_map/reshape | solution.py:18
  13.9 0.0 copy-done.1
  13.9 0.1 broadcast_maximum_fusion.1
  14.0 0.7 reshape.46
  14.7 0.4 convert_reduce_fusion
  15.1 0.4 reduce_window_sum.23
  15.5 13.3 %all_gather.10 = f32[4,2,112]{2,1,0:T(2,128)S(1)} all-gather(f32[1,2,112]{2,1,0:T(2,128)S(1)} %broadcast_in_dim.41), channel_id=1, replica_groups=mesh['groups'=2,'frames'=4,'heads'=4] {'frames'}, dimensions={0}, use_global_device_ids=true | all-gather | bytes 4480 | tf_op jit(solution)/shard_map/all_gather | solution.py:28
  28.8 0.1 select_reduce_fusion.1
  28.9 0.1 fusion.12
  29.0 0.1 copy.16
  29.1 1.8 %fusion.17 = (f32[2,112,112]{2,1,0:T(8,128)S(1)}, f32[4,2,112,112]{3,2,1,0:T(8,128)S(1)}) fusion(bf16[4,512,2,112]{1,0,3,2:T(4,128)(2,1)} %reshape.47, bf16[4,512,2,112]{1,0,3,2:T(4,128)(2,1)S(1)} %reshape.46), kind=kOutput, calls=%fused_computation.36 | convolution fusion | flops 102835712 | bytes 2336768 | tf_op jit(solution)/shard_map/fthi,fthj->fhij/dot_general | solution.py:19
  30.9 19.9 %all-gather = f32[8,112,112]{2,1,0:T(8,128)S(1)} all-gather(f32[2,112,112]{2,1,0:T(8,128)S(1)} %get-tuple-element.5), channel_id=2, replica_groups=mesh['groups'=2,'frames'=4,'heads'=4] {'frames'}, dimensions={0}, use_global_device_ids=true | all-gather | bytes 501760 | tf_op jit(solution)/shard_map/all_gather | solution.py:27
  50.8 0.1 select_reduce_fusion
  50.9 0.4 fusion.7
  51.3 0.1 fusion.3
  51.3 1.4 %fusion.2 = bf16[4,512,2,112]{1,3,2,0:T(8,128)(2,1)} fusion(bf16[4,2,112,112]{3,2,1,0:T(8,128)(2,1)S(1)} %fusion.3, f32[4,512,2]{1,2,0:T(2,128)S(1)} %fusion.13, bf16[4,512,2,112]{1,0,3,2:T(4,128)(2,1)S(1)} %reshape.48), kind=kOutput, calls=%fused_computation.4 | convolution fusion | flops 103677952 | bytes 2052096 | tf_op jit(solution)/shard_map/fthi,fhij->fthj/dot_general | solution.py:38
  52.7 0.0 copy-start.2
  52.7 3.6 %all-to-all-start = ((bf16[4,512,224]{1,2,0:T(8,128)(2,1)}), bf16[4,512,224]{1,2,0:T(8,128)(2,1)S(1)}, u32[]{:S(2)}, u32[]{:S(2)}) async-start(bf16[4,512,224]{1,2,0:T(8,128)(2,1)} %bitcast.5), calls=%async_computation | async-start | bytes 1835008 | tf_op jit(solution)/shard_map/all_to_all | solution.py:57
  56.4 0.0 copy-done
  56.4 4.1 %fusion.10 = f32[512,2240]{0,1:T(8,128)} fusion(f32[4,2240]{1,0:T(4,128)S(1)} %copy-done, s32[512]{0:T(512)S(1)} %add_select_fusion), kind=kOutput, calls=%fused_computation.19 | convolution fusion | flops 55052288 | bytes 4625408 | tf_op jit(solution)/shard_map/dot_general | solution.py:54
  60.5 8.8 %all-to-all-done = bf16[4,512,224]{1,2,0:T(8,128)(2,1)S(1)} async-done(((bf16[4,512,224]{1,2,0:T(8,128)(2,1)}), bf16[4,512,224]{1,2,0:T(8,128)(2,1)S(1)}, u32[]{:S(2)}, u32[]{:S(2)}) %all-to-all-start) | async-done | bytes 917536 | tf_op jit(solution)/shard_map/all_to_all | solution.py:57
  69.4 29.2 %all-gather.3.cloned.1.call-done = bf16[896,2240]{1,0:T(8,128)(2,1)} async-done(((bf16[224,2240]{1,0:T(8,128)(2,1)}), bf16[896,2240]{1,0:T(8,128)(2,1)}) %all-gather.3.cloned.1.call-update) | async-done | bytes 4014096 | tf_op jit(solution)/shard_map/all_gather | solution.py:60
  98.6 0.0 copy-done.2
  98.6 7.8 %fusion.1 = bf16[512,2240]{0,1:T(8,128)(2,1)} fusion(f32[512,2240]{0,1:T(8,128)} %fusion.10, bf16[512,896]{0,1:T(8,128)(2,1)S(1)} %bitcast.30, bf16[896,2240]{1,0:T(8,128)(2,1)} %all-gather.3.cloned.1.call-done, bf16[512,2240]{0,1:T(8,128)(2,1)S(1)} %copy-done.2), kind=kOutput, calls=%fused_computation.2 | convolution fusion | flops 2059796480 | bytes 14106624 | tf_op jit(solution)/shard_map/dot_general | solution.py:58
  (3 shorter events, 0.0 us)
Async XLA Ops:
  6.5 49.9 %copy-start = (f32[4,2240]{1,0:T(4,128)S(1)}, f32[4,2240]{1,0:T(4,128)}, u32[]{:S(2)}) copy-start(f32[4,2240]{1,0:T(4,128)} %param.11) | copy-start | bytes 107524
  6.5 7.4 %copy-start.1 = (bf16[2048,224]{0,1:T(8,128)(2,1)S(1)}, bf16[2048,224]{0,1:T(8,128)(2,1)}, u32[]{:S(2)}) copy-start(bf16[2048,224]{0,1:T(8,128)(2,1)} %param.7) | copy-start | bytes 2752516
  6.5 92.0 %all-gather.3.cloned.1.call-start = ((), (), s32[]{:S(2)}) async-start(), calls=%async_computation.1 | async-start | bytes 5160960 | tf_op jit(solution)/shard_map/all_gather | solution.py:60
  52.7 45.9 %copy-start.2 = (bf16[512,2240]{0,1:T(8,128)(2,1)S(1)}, bf16[512,2240]{0,1:T(8,128)(2,1)}, u32[]{:S(2)}) copy-start(bf16[512,2240]{0,1:T(8,128)(2,1)} %param.9) | copy-start | bytes 6881284
  52.7 16.6 %all-to-all-start = ((bf16[4,512,224]{1,2,0:T(8,128)(2,1)}), bf16[4,512,224]{1,2,0:T(8,128)(2,1)S(1)}, u32[]{:S(2)}, u32[]{:S(2)}) async-start(bf16[4,512,224]{1,2,0:T(8,128)(2,1)} %bitcast.5), calls=%async_computation | async-start | bytes 1835008 | tf_op jit(solution)/shard_map/all_to_all | solution.py:57
Sparse Core Ops, SparseCore 0:
  8.9 89.6 all-gather.2
where the time goes:
time: 114 us; the launch traced here: 113 us
  waiting for transfers between devices  38.8 us (34%)
  blocking collectives  33.1 us (29%)
  matrix products  15.5 us (14%)
  between operations  13.5 us (12%)
  local copies, waits for them, and re-layouts  4.76 us (4%)
  other arithmetic  3.95 us (3%)
  starting transfers between devices  3.64 us (3%)
    all_gather x1, waiting for transfers between devices, per_device(): lax.all_gather(out_proj, 'frames', axis=0, tiled=True)  29.2 us
    all_gather x1, blocking collectives, per_device(): lax.all_gather(own_state[None], 'frames', axis=0, tiled=True)  19.9 us
    all_gather x1, blocking collectives, per_device(): lax.all_gather(own_sum[None], 'frames', axis=0, tiled=True)  13.3 us
    all_to_all x1, waiting for transfers between devices, per_device(): lax.all_to_all(attended, 'heads', split_axis=0, concat_axis=1, tiled=True)  8.84 us
    dot_general x1, matrix products, per_device(): jnp.dot(token_rows, lax.all_gather(out_proj, 'frames', axis=0, tiled=True...  7.75 us
    dot_general x1, matrix products, per_device(): jnp.dot(selector, frame_gate, precision=lax.Precision.HIGHEST, preferred_...  4.13 us
    all_to_all x1, starting transfers between devices, per_device(): lax.all_to_all(attended, 'heads', split_axis=0, concat_axis=1, tiled=True)  3.64 us
    reshape x1, local copies, waits for them, and re-layouts, per_device(): value_frames = value_heads.reshape(block_shape)  3.23 us
  transfers between devices with their start and end apart: 2, of which 2 were waited for; matrix products, arithmetic and copies ran while one was open for 14% of the time, Pallas kernels for 0%

commit v1 on v0

--- a/solution.py
+++ b/solution.py
@@ -1,3 +1,4 @@
+import functools
 import jax
 import jax.numpy as jnp
 from jax import lax
@@ -7,6 +8,37 @@
 HEADS_DEV = 2
 FRAME_TOK = 512
 EPSILON = 1e-06
+
+
+def _close_roots(field_in, which_axis, array_dim):
+    h_now = lax.axis_size(which_axis)
+    piece_now, res, a_next = (h_now, lax.axis_index(which_axis), field_in.shape[array_dim])
+    gallery = []
+    for dev_i, p in enumerate(field_in.shape):
+        gallery.append(p * piece_now if dev_i == array_dim else p)
+    b_now = jnp.zeros(gallery, field_in.dtype)
+    arr_next = lax.dynamic_update_slice_in_dim(b_now, field_in, res * a_next, axis=array_dim)
+    met_up = tmp = field_in
+    for rr in range(1, piece_now // 2 + 1):
+        grid = []
+        for dev_i in range(piece_now):
+            grid.append((dev_i, (dev_i + 1) % piece_now))
+        met_up = lax.ppermute(met_up, which_axis, grid)
+        arr_next = lax.dynamic_update_slice_in_dim(
+            arr_next, met_up, (res - rr) % piece_now * a_next, axis=array_dim
+        )
+        if 2 * rr < piece_now:
+            all_rows = []
+            for dev_i in range(piece_now):
+                all_rows.append((dev_i, (dev_i - 1) % piece_now))
+            tmp = lax.ppermute(tmp, which_axis, all_rows)
+            arr_next = lax.dynamic_update_slice_in_dim(
+                arr_next, tmp, (res + rr) % piece_now * a_next, axis=array_dim
+            )
+    return arr_next
+
+
+detail_area = functools.partial(_close_roots, which_axis="frames", array_dim=0)
 
 
 def per_device(query_heads, key_heads, value_heads, residual, out_proj, frame_gate):
@@ -24,7 +56,7 @@
     own_sum = jnp.sum(frame_sum, axis=0)
     position = lax.axis_index("frames")
     gathered = (
-        lax.all_gather(own_state[None], "frames", axis=0, tiled=True),
+        detail_area(own_state[None]),
         lax.all_gather(own_sum[None], "frames", axis=0, tiled=True),
     )
     pieces = gathered[0].shape[0]

time: 114 us -> 110 us (0.965)
  blocking collectives: 33.1 us -> 9.95 us
  waiting for transfers between devices: 38.8 us -> 52.5 us
  starting transfers between devices: 3.64 us -> 8.9 us
    all_gather x1 -> x0, blocking collectives: 19.9 us -> none  [per_device(): lax.all_gather(own_state[None], 'frames', axis=0, tiled=True)]
    ppermute x0 -> x3, waiting for transfers between devices: none -> 8.29 us  [the longest x2 8.28 us: _close_roots(): met_up = lax.ppermute(met_up, which_axis, grid)]
    all_gather x1, waiting for transfers between devices: 29.2 us -> 34.7 us  [per_device(): lax.all_gather(out_proj, 'frames', axis=0, tiled=True)]
    ppermute x0 -> x3, starting transfers between devices: none -> 5.25 us  [the longest x2 3.16 us: _close_roots(): met_up = lax.ppermute(met_up, which_axis, grid)]
    all_gather x1, blocking collectives: 13.3 us -> 9.95 us  [per_device(): lax.all_gather(own_sum[None], 'frames', axis=0, tiled=True)]
    max x1, other arithmetic: 1.24 us -> 0.06 us  [per_device(): query_pos = jnp.maximum(query_heads, 0).reshape(block_shape)]
    reduce_sum x1, other arithmetic: 1.44 us -> 0.26 us  [per_device(): own_sum = jnp.sum(frame_sum, axis=0)]
    max x1, other arithmetic: 0.06 us -> 1.24 us  [per_device(): key_pos = jnp.maximum(key_heads, 0).reshape(block_shape)]
  transfers between devices with their start and end apart: 2 -> 5, of which waited for: 2 -> 3; matrix products, arithmetic and copies ran while one was open for 14% -> 15% of each run, Pallas kernels for 0% -> 0%
where the time goes in v1:
time: 110 us; the launch traced here: 109 us
  waiting for transfers between devices  52.5 us (48%)
  matrix products  15.6 us (14%)
  between operations  13.6 us (12%)
  blocking collectives  9.95 us (9%)
  starting transfers between devices  8.9 us (8%)
  local copies, waits for them, and re-layouts  5.84 us (5%)
  other arithmetic  3.02 us (3%)
    all_gather x1, waiting for transfers between devices, per_device(): lax.all_gather(out_proj, 'frames', axis=0, tiled=True)  34.7 us
    all_gather x1, blocking collectives, per_device(): lax.all_gather(own_sum[None], 'frames', axis=0, tiled=True)  9.95 us
    all_to_all x1, waiting for transfers between devices, per_device(): lax.all_to_all(attended, 'heads', split_axis=0, concat_axis=1, tiled=True)  8.83 us
    ppermute x2, waiting for transfers between devices, _close_roots(): met_up = lax.ppermute(met_up, which_axis, grid)  8.28 us
    dot_general x1, matrix products, per_device(): jnp.dot(token_rows, lax.all_gather(out_proj, 'frames', axis=0, tiled=True...  7.75 us
    dot_general x1, matrix products, per_device(): jnp.dot(selector, frame_gate, precision=lax.Precision.HIGHEST, preferred_...  4.13 us
    all_to_all x1, starting transfers between devices, per_device(): lax.all_to_all(attended, 'heads', split_axis=0, concat_axis=1, tiled=True)  3.64 us
    reshape x1, local copies, waits for them, and re-layouts, per_device(): value_frames = value_heads.reshape(block_shape)  3.3 us
  transfers between devices with their start and end apart: 5, of which 3 were waited for; matrix products, arithmetic and copies ran while one was open for 15% of the time, Pallas kernels for 0%

profile of v1, /device:TPU:0, one launch (start us, length us, event | category | flops | bytes accessed | tf_op | source)
XLA Modules:
  0.0 109.4 jit_solution(10255176279395094350)
XLA Ops:
  6.5 0.0 copy-start
  6.5 0.0 all-gather.2.cloned.1.call-start
  6.5 0.7 all-gather.2.cloned.1.call-update
  7.3 0.0 copy-start.1
  7.3 3.3 %reshape.47 = bf16[4,512,2,112]{1,0,3,2:T(4,128)(2,1)} reshape(bf16[2048,224]{0,1:T(8,128)(2,1)} %param.8) | data formatting | bytes 1835008 | tf_op jit(solution)/shard_map/reshape | solution.py:50
  10.6 1.2 %broadcast_maximum_fusion.1 = bf16[2048,224]{0,1:T(8,128)(2,1)S(1)} fusion(bf16[2048,224]{0,1:T(8,128)(2,1)} %param.7), kind=kLoop, calls=%fused_computation.16 | loop fusion | flops 458752 | bytes 1835008 | tf_op jit(solution)/shard_map/max | solution.py:49
  11.8 0.7 reshape.46
  12.5 0.0 copy-start.2
  12.5 1.9 %fusion.17 = (f32[2,112,112]{2,1,0:T(8,128)S(1)}, f32[4,2,112,112]{3,2,1,0:T(8,128)S(1)}) fusion(bf16[4,512,2,112]{1,0,3,2:T(4,128)(2,1)} %reshape.47, bf16[4,512,2,112]{1,0,3,2:T(4,128)(2,1)S(1)} %reshape.46), kind=kOutput, calls=%fused_computation.40 | convolution fusion | flops 102835712 | bytes 2336768 | tf_op jit(solution)/shard_map/fthi,fthj->fhij/dot_general | solution.py:51
  14.4 3.1 %collective-permute-start = (f32[1,2,112,112]{3,2,1,0:T(8,128)S(1)}, f32[1,2,112,112]{3,2,1,0:T(8,128)S(1)}, u32[]{:S(2)}, u32[]{:S(2)}) collective-permute-start(f32[1,2,112,112]{3,2,1,0:T(8,128)S(1)} %bitcast.30), channel_id=1, source_target_pairs={{0,4},{4,8},{8,12},{12,0},{1,5},{5,9},{9,13},{13,1},{2,6},{6,10},{... | collective-permute-start | bytes 301064 | tf_op jit(solution)/shard_map/ppermute | solution.py:26
  17.5 2.1 %collective-permute-start.1 = (f32[1,2,112,112]{3,2,1,0:T(8,128)S(1)}, f32[1,2,112,112]{3,2,1,0:T(8,128)}, u32[]{:S(2)}, u32[]{:S(2)}) collective-permute-start(f32[1,2,112,112]{3,2,1,0:T(8,128)S(1)} %bitcast.31), channel_id=1, source_target_pairs={{0,12},{4,0},{8,4},{12,8},{1,13},{5,1},{9,5},{13,9},{2,14},{6,2},{... | collective-permute-start | bytes 301064 | tf_op jit(solution)/shard_map/ppermute | solution.py:34
  19.6 0.0 copy-done.1
  19.6 0.3 convert_reduce_fusion.1
  19.9 0.1 broadcast_in_dim.42
  19.9 0.0 copy-done.2
  19.9 0.1 broadcast_maximum_fusion
  20.0 0.7 reshape.48
  20.7 0.4 convert_reduce_fusion
  21.1 0.4 reduce_window_sum.23
  21.5 10.0 %all_gather.6 = f32[4,2,112]{2,1,0:T(2,128)S(1)} all-gather(f32[1,2,112]{2,1,0:T(2,128)S(1)} %broadcast_in_dim.42), channel_id=1, replica_groups=mesh['groups'=2,'frames'=4,'heads'=4] {'frames'}, dimensions={0}, use_global_device_ids=true | all-gather | bytes 4480 | tf_op jit(solution)/shard_map/all_gather | solution.py:60
  31.5 0.1 select_reduce_fusion.1
  31.6 0.1 fusion.12
  31.7 0.1 copy.20
  31.8 0.3 fusion.18
  32.2 0.4 fusion.6
  32.6 0.0 collective-permute-done
  32.6 0.1 collective-permute-start.2
  32.7 0.0 collective-permute-done.1
  32.7 0.9 constant_dynamic-update-slice_fusion.1
  33.6 8.3 %collective-permute-done.2 = f32[1,2,112,112]{3,2,1,0:T(8,128)S(1)} collective-permute-done((f32[1,2,112,112]{3,2,1,0:T(8,128)S(1)}, f32[1,2,112,112]{3,2,1,0:T(8,128)S(1)}, u32[]{:S(2)}, u32[]{:S(2)}) %collective-permute-start.2) | collective-permute-done | bytes 100384 | tf_op jit(solution)/shard_map/ppermute | solution.py:26
  41.9 0.1 select_reduce_fusion
  42.0 1.4 %fusion.2 = bf16[4,512,2,112]{1,3,2,0:T(8,128)(2,1)} fusion(f32[4,512,2]{1,2,0:T(2,128)S(1)} %fusion.13, bf16[4,512,2,112]{1,0,3,2:T(4,128)(2,1)S(1)} %reshape.48, f32[4,2,112,112]{3,2,1,0:T(8,128)S(1)} %fusion.18, f32[2,112,112]{2,1,0:T(8,128)S(1)} %select_reduce_fusion), kind=kOutput, calls=%fused_computation.4 | convolution fusion | flops 103878656 | bytes 2353152 | tf_op jit(solution)/shard_map/fthi,fhij->fthj/dot_general | solution.py:70
  43.5 0.0 copy-start.3
  43.5 3.6 %all-to-all-start = ((bf16[4,512,224]{1,2,0:T(8,128)(2,1)}), bf16[4,512,224]{1,2,0:T(8,128)(2,1)S(1)}, u32[]{:S(2)}, u32[]{:S(2)}) async-start(bf16[4,512,224]{1,2,0:T(8,128)(2,1)} %bitcast.5), calls=%async_computation | async-start | bytes 1835008 | tf_op jit(solution)/shard_map/all_to_all | solution.py:89
  47.1 0.0 copy-done
  47.1 4.1 %fusion.9 = f32[512,2240]{0,1:T(8,128)} fusion(f32[4,2240]{1,0:T(4,128)S(1)} %copy-done, s32[512]{0:T(512)S(1)} %add_select_fusion), kind=kOutput, calls=%fused_computation.18 | convolution fusion | flops 55052288 | bytes 4625408 | tf_op jit(solution)/shard_map/dot_general | solution.py:86
  51.3 8.8 %all-to-all-done = bf16[4,512,224]{1,2,0:T(8,128)(2,1)S(1)} async-done(((bf16[4,512,224]{1,2,0:T(8,128)(2,1)}), bf16[4,512,224]{1,2,0:T(8,128)(2,1)S(1)}, u32[]{:S(2)}, u32[]{:S(2)}) %all-to-all-start) | async-done | bytes 917536 | tf_op jit(solution)/shard_map/all_to_all | solution.py:89
  60.1 34.7 %all-gather.2.cloned.1.call-done = bf16[896,2240]{1,0:T(8,128)(2,1)} async-done(((bf16[224,2240]{1,0:T(8,128)(2,1)}), bf16[896,2240]{1,0:T(8,128)(2,1)}) %all-gather.2.cloned.1.call-update) | async-done | bytes 4014096 | tf_op jit(solution)/shard_map/all_gather | solution.py:92
  94.8 0.0 copy-done.3
  94.8 7.8 %fusion.1 = bf16[512,2240]{0,1:T(8,128)(2,1)} fusion(f32[512,2240]{0,1:T(8,128)} %fusion.9, bf16[512,896]{0,1:T(8,128)(2,1)S(1)} %bitcast.29, bf16[896,2240]{1,0:T(8,128)(2,1)} %all-gather.2.cloned.1.call-done, bf16[512,2240]{0,1:T(8,128)(2,1)S(1)} %copy-done.3), kind=kOutput, calls=%fused_computation.2 | convolution fusion | flops 2059796480 | bytes 14106624 | tf_op jit(solution)/shard_map/dot_general | solution.py:90
  (7 shorter events, 0.1 us)
Async XLA Ops:
  6.5 40.6 %copy-start = (f32[4,2240]{1,0:T(4,128)S(1)}, f32[4,2240]{1,0:T(4,128)}, u32[]{:S(2)}) copy-start(f32[4,2240]{1,0:T(4,128)} %param.11) | copy-start | bytes 107524
  6.5 88.2 %all-gather.2.cloned.1.call-start = ((), (), s32[]{:S(2)}) async-start(), calls=%async_computation.1 | async-start | bytes 5160960 | tf_op jit(solution)/shard_map/all_gather | solution.py:92
  7.3 12.3 %copy-start.1 = (bf16[2048,224]{0,1:T(8,128)(2,1)S(1)}, bf16[2048,224]{0,1:T(8,128)(2,1)}, u32[]{:S(2)}) copy-start(bf16[2048,224]{0,1:T(8,128)(2,1)} %param.7) | copy-start | bytes 2752516
  12.5 7.5 %copy-start.2 = (bf16[2048,224]{0,1:T(8,128)(2,1)S(1)}, bf16[2048,224]{0,1:T(8,128)(2,1)}, u32[]{:S(2)}) copy-start(bf16[2048,224]{0,1:T(8,128)(2,1)} %param.6) | copy-start | bytes 2752516
  14.4 18.2 %collective-permute-start = (f32[1,2,112,112]{3,2,1,0:T(8,128)S(1)}, f32[1,2,112,112]{3,2,1,0:T(8,128)S(1)}, u32[]{:S(2)}, u32[]{:S(2)}) collective-permute-start(f32[1,2,112,112]{3,2,1,0:T(8,128)S(1)} %bitcast.30), channel_id=1, source_target_pairs={{0,4},{4,8},{8,12},{12,0},{1,5},{5,9},{9,13},{13,1},{2,6},{6,10},{... | collective-permute-start | bytes 301064 | tf_op jit(solution)/shard_map/ppermute | solution.py:26
  17.5 15.2 %collective-permute-start.1 = (f32[1,2,112,112]{3,2,1,0:T(8,128)S(1)}, f32[1,2,112,112]{3,2,1,0:T(8,128)}, u32[]{:S(2)}, u32[]{:S(2)}) collective-permute-start(f32[1,2,112,112]{3,2,1,0:T(8,128)S(1)} %bitcast.31), channel_id=1, source_target_pairs={{0,12},{4,0},{8,4},{12,8},{1,13},{5,1},{9,5},{13,9},{2,14},{6,2},{... | collective-permute-start | bytes 301064 | tf_op jit(solution)/shard_map/ppermute | solution.py:34
  32.6 9.3 %collective-permute-start.2 = (f32[1,2,112,112]{3,2,1,0:T(8,128)S(1)}, f32[1,2,112,112]{3,2,1,0:T(8,128)S(1)}, u32[]{:S(2)}, u32[]{:S(2)}) collective-permute-start(f32[1,2,112,112]{3,2,1,0:T(8,128)S(1)} %collective-permute-done), channel_id=1, source_target_pairs={{0,4},{4,8},{8,12},{12,0},{1,5},{5,9},{9,13},{13,1},{2,6},{6,10},{... | collective-permute-start | bytes 301064 | tf_op jit(solution)/shard_map/ppermute | solution.py:26
  43.5 51.3 %copy-start.3 = (bf16[512,2240]{0,1:T(8,128)(2,1)S(1)}, bf16[512,2240]{0,1:T(8,128)(2,1)}, u32[]{:S(2)}) copy-start(bf16[512,2240]{0,1:T(8,128)(2,1)} %param.9) | copy-start | bytes 6881284
  43.5 16.6 %all-to-all-start = ((bf16[4,512,224]{1,2,0:T(8,128)(2,1)}), bf16[4,512,224]{1,2,0:T(8,128)(2,1)S(1)}, u32[]{:S(2)}, u32[]{:S(2)}) async-start(bf16[4,512,224]{1,2,0:T(8,128)(2,1)} %bitcast.5), calls=%async_computation | async-start | bytes 1835008 | tf_op jit(solution)/shard_map/all_to_all | solution.py:89
Sparse Core Ops, SparseCore 0:
  8.9 85.8 all-gather.1
